TPU v7x, 256 devices: a whole 4x4x8 slice. The times are simulated.
256 devices in a mesh: member: 4 (over z_hi), token: 64 (over z_lo, x, y, core).
Axes of the slice: x: 4, y: 4, z: 8 (z_hi: 4, z_lo: 2; z = z_hi * 2 + z_lo), core: 2. Of those that a mesh axis runs over, the one named last changes fastest.
Arguments:
- members_in: bfloat16 [8, 8192, 1024], P('member', 'token'), may hold values from -16 to 16
- member_noise: bfloat16 [8, 8192, 1024], P('member', 'token'), may hold values from -6 to 6
- norm_gain: float32 [1024], replicated, may hold values from 0.25 to 1.75
- weight_query: bfloat16 [1024, 1024], replicated, may hold values from -0.1875 to 0.1875
- weight_key: bfloat16 [1024, 1024], replicated, may hold values from -0.1875 to 0.1875
- weight_value: bfloat16 [1024, 1024], replicated, may hold values from -0.1875 to 0.1875
- weight_out: bfloat16 [1024, 1024], replicated, may hold values from -0.1875 to 0.1875
- decoder_projection_weight: bfloat16 [100, 1024], replicated, may hold values from -0.1875 to 0.1875
- decoder_bias: float32 [100], replicated, may hold values from -3 to 3
- observations: float32 [100, 65536], P(None, 'token'), may hold values from -6 to 6
- surface_extent_factor: float32 [65536], P('token'), may hold values from 0.3 to 3
- quantity_scoring_factor: float32 [100], replicated, may hold values from 0.2 to 2
- point_map: int32 [65536], P('token'), may hold values from 0 to 127
Outputs:
- mean_scoring: float32 [], replicated
- grad_members: bfloat16 [8, 8192, 1024], P('member', 'token')
- grad_out: float32 [1024, 1024], P('token')
- grad_decoder: float32 [100, 1024], replicated
Inputs may be any that keep to these rules, and one draw needn't show every extreme that they name: Point p belongs to token (p // 1024) * 128 + point_map[p].
All inputs are finite; a program needn't handle non-finite values.
Results may differ from a plain program's by a relative error of at most 0.015.
Values may be sent and summed in bfloat16 or wider, within the bound.
No kernel may reach another device: no remote copies, remote signals or barrier semaphores. Data moves between devices by JAX's collectives and lax.ppermute only.
A program may use at most 128 MiB of HBM per device.

v0:
```python
import jax
import jax.numpy as jnp
from jax import lax
from jax.sharding import PartitionSpec as P

HEADS = 16
HALF = 128
EPSILON = 1e-06
SMOOTH = 0.01


def extended_2(block, sides, width):
    for axis, dim in sides:
        count = lax.axis_size(axis)
        forward = [(i, i + 1) for i in range(count - 1)]
        backward = [(target, source) for source, target in forward]
        low = lax.ppermute(
            lax.slice_in_dim(block, block.shape[dim] - width, None, axis=dim), axis, forward
        )
        high = lax.ppermute(lax.slice_in_dim(block, 0, width, axis=dim), axis, backward)
        block = jnp.concatenate([low, block, high], axis=dim)
    return block


def from_behind(block, axis, distance):
    devices = range(lax.axis_size(axis))
    route = [(i - distance, i) for i in devices if i - distance in devices]
    return lax.ppermute(block, axis, route)


def normalize_heads(flat):
    rows, width = flat.shape
    split = flat.reshape(rows, HEADS, width // HEADS)
    split = split * lax.rsqrt(jnp.mean(split * split, axis=-1, keepdims=True) + EPSILON)
    return split.reshape(rows, width)


def project(state_in, member_noise, norm_gain, weight_query, weight_key, weight_value):
    member_rows, tokens, width = state_in.shape
    mixed = state_in + member_noise.astype(jnp.float32)
    normed = (
        mixed * lax.rsqrt(jnp.mean(mixed * mixed, axis=-1, keepdims=True) + EPSILON) * norm_gain
    ).astype(jnp.bfloat16)
    flat = normed.reshape(member_rows * tokens, width)
    query = normalize_heads(jnp.dot(flat, weight_query, preferred_element_type=jnp.float32)).astype(
        jnp.bfloat16
    )
    key = normalize_heads(jnp.dot(flat, weight_key, preferred_element_type=jnp.float32)).astype(
        jnp.bfloat16
    )
    value = jnp.dot(flat, weight_value, preferred_element_type=jnp.float32).astype(jnp.bfloat16)
    full_shape = (member_rows, tokens, width)
    return (query.reshape(full_shape), key.reshape(full_shape), value.reshape(full_shape))


def attend(query, keys, values, leading_realization, total):
    member_rows, queries, width = query.shape
    realization_number = keys.shape[1]
    depth = width // HEADS
    query_heads = query.reshape(member_rows, queries, HEADS, depth)
    key_heads = keys.reshape(member_rows, realization_number, HEADS, depth)
    value_heads = values.reshape(member_rows, realization_number, HEADS, depth)
    scores = jnp.einsum(
        "mqhd,mkhd->mhqk", query_heads, key_heads, preferred_element_type=jnp.float32
    ) / jnp.sqrt(jnp.float32(depth))
    query_pos = leading_realization + lax.iota(jnp.int32, queries)
    key_pos = leading_realization - HALF + lax.iota(jnp.int32, realization_number)
    allowed = (key_pos[None, :] >= query_pos[:, None] - HALF) & (
        key_pos[None, :] < query_pos[:, None] + HALF
    )
    allowed = allowed & (key_pos[None, :] >= 0) & (key_pos[None, :] < total)
    raised = jnp.where(allowed[None, None], jnp.exp(scores), jnp.float32(0.0))
    probs = (raised / jnp.sum(raised, axis=-1, keepdims=True)).astype(jnp.bfloat16)
    mixed = jnp.einsum("mhqk,mkhd->mqhd", probs, value_heads, preferred_element_type=jnp.float32)
    return mixed.reshape(member_rows, queries, width).astype(jnp.bfloat16)


def softened_magnitude(diff):
    return jnp.sqrt(diff * diff + SMOOTH)


def unbiased_ranked_score(
    realization_prediction, observed_grid, surface_extent, quantity_scoring_factor
):
    realization_number = realization_prediction.shape[0]
    accuracy_part = softened_magnitude(realization_prediction[0] - observed_grid)
    for realization_position in range(1, realization_number):
        accuracy_part = accuracy_part + softened_magnitude(
            realization_prediction[realization_position] - observed_grid
        )
    dispersion_part = jnp.zeros_like(accuracy_part)
    for leading_realization in range(realization_number):
        for paired_realization in range(leading_realization + 1, realization_number):
            dispersion_part = dispersion_part + softened_magnitude(
                realization_prediction[leading_realization]
                - realization_prediction[paired_realization]
            )
    score = accuracy_part / realization_number - dispersion_part / (
        realization_number * (realization_number - 1)
    )
    return jnp.sum(quantity_scoring_factor[:, None] * surface_extent[None, :] * score)


def shards(
    members_in,
    member_noise,
    norm_gain,
    weight_query,
    weight_key,
    weight_value,
    weight_out,
    decoder_projection_weight,
    decoder_bias,
    observations,
    surface_extent_factor,
    quantity_scoring_factor,
    point_map,
):
    member_rows, tokens, width = members_in.shape
    state = members_in.astype(jnp.float32)

    def front(state_in):
        return project(state_in, member_noise, norm_gain, weight_query, weight_key, weight_value)

    (query, key, value), front_pull = jax.vjp(front, state)
    stacked = jnp.stack([key, value])
    extended = extended_2(stacked, (("token", 2),), HALF)
    leading_realization = lax.axis_index("token") * tokens
    total = tokens * lax.axis_size("token")

    def middle(query_in, extended_in):
        return attend(query_in, extended_in[0], extended_in[1], leading_realization, total)

    attended, middle_pull = jax.vjp(middle, query, extended)
    flat_att = attended.reshape(member_rows * tokens, width)
    update = jnp.dot(flat_att, weight_out, preferred_element_type=jnp.float32).reshape(
        member_rows, tokens, width
    )
    residual_stream_state = (state + member_noise.astype(jnp.float32) + update).astype(jnp.bfloat16)

    def decode_tokens(residual_in, decoder_in):
        mapping_array = jnp.einsum(
            "vc,mtc->mvt",
            decoder_in.astype(jnp.bfloat16),
            residual_in,
            preferred_element_type=jnp.float32,
        )
        mapping_array = mapping_array + decoder_bias[None, :, None]
        return jnp.take(mapping_array, point_map, axis=2)

    realization_prediction, readout_slope_pulled = jax.vjp(
        decode_tokens, residual_stream_state, decoder_projection_weight.astype(jnp.float32)
    )
    location_places = realization_prediction.shape[2]
    groups = lax.axis_size("member")
    local_shard = lax.axis_index("member")
    gathered_lines = lax.all_gather(realization_prediction, "member", axis=0, tiled=True)

    def score_all(whole):
        return unbiased_ranked_score(
            whole, observations, surface_extent_factor, quantity_scoring_factor
        )

    full_loss, score_pull = jax.vjp(score_all, gathered_lines)
    (complete_gradient,) = score_pull(jnp.ones((), jnp.float32))
    prediction_slope = lax.dynamic_slice_in_dim(
        complete_gradient, local_shard * member_rows, member_rows, 0
    )
    partial_loss = full_loss / groups
    carried_slope, readout_piece_result = readout_slope_pulled(prediction_slope)
    overall_scoring_amount, grad_decoder = lax.psum(
        (partial_loss, readout_piece_result), ("member", "token")
    )
    mean_scoring = overall_scoring_amount / (
        realization_prediction.shape[1] * location_places * lax.axis_size("token")
    )
    flat_grad = carried_slope.reshape(member_rows * tokens, width)
    grad_attended = (
        jnp.dot(flat_grad, weight_out.T, preferred_element_type=jnp.float32)
        .astype(jnp.bfloat16)
        .reshape(member_rows, tokens, width)
    )
    grad_query, grad_extended = middle_pull(grad_attended)
    lower_rim = grad_extended[:, :, :HALF]
    upper_rim = grad_extended[:, :, tokens + HALF :]
    inner = grad_extended[:, :, HALF : tokens + HALF].astype(jnp.float32)
    from_next = from_behind(lower_rim, "token", -1)
    from_prev = from_behind(upper_rim, "token", 1)
    inner = inner.at[:, :, tokens - HALF :].add(from_next.astype(jnp.float32))
    inner = inner.at[:, :, :HALF].add(from_prev.astype(jnp.float32))
    (grad_front,) = front_pull(
        (grad_query, inner[0].astype(jnp.bfloat16), inner[1].astype(jnp.bfloat16))
    )
    grad_members = (grad_front + carried_slope.astype(jnp.float32)).astype(jnp.bfloat16)
    contract = (((0,), (0,)), ((), ()))
    product = lax.dot_general(flat_att, flat_grad, contract, preferred_element_type=jnp.float32)
    summed = lax.psum(product.astype(jnp.bfloat16), "member").astype(jnp.float32)
    grad_out = lax.psum_scatter(summed, "token", scatter_dimension=0, tiled=True)
    return (mean_scoring, grad_members, grad_out, grad_decoder)


def solution(mesh):
    return jax.shard_map(
        shards,
        mesh=mesh,
        in_specs=(
            P("member", "token", None),
            P("member", "token", None),
            P(),
            P(),
            P(),
            P(),
            P(),
            P(),
            P(),
            P(None, "token"),
            P("token"),
            P(),
            P("token"),
        ),
        out_specs=(P(), P("member", "token", None), P("token", None), P()),
        check_vma=False,
    )
```

profile of v0, /device:TPU:64, one launch (start us, length us, event | category | flops | bytes accessed | tf_op | source)
XLA Modules:
  0.0 912.2 jit_solution(12834779146447870691)
XLA Ops:
  7.3 1.6 multiply_reduce_fusion.3
  8.9 3.9 copy.95
  13.0 0.8 copy-done.26
  13.8 2.3 multiply_reduce_fusion.2
  17.4 0.9 multiply_convert_fusion.1
  18.3 2.0 convert_element_type.154
  20.3 3.3 convolution_convert_fusion.8
  23.5 2.0 copy.96
  25.5 3.8 pad_maximum_fusion.1
  29.3 2.8 collective-permute-start
  32.1 1.6 collective-permute-start.1
  33.7 3.9 copy.98
  37.7 2.6 multiply_reduce_fusion.1
  40.9 5.7 pad_maximum_fusion
  46.5 2.2 fusion.223
  49.2 1.8 fusion.7
  51.1 1.3 divide_convert_fusion
  52.4 1.3 copy-done.11
  53.7 1.5 convolution_convert_fusion.5
  56.0 0.8 copy-done.17
  56.8 0.9 fusion.22
  57.8 1.0 copy.102
  58.8 7.5 gather_fusion
  66.3 6.1 select_bitcast_fusion
  72.4 2.3 copy.103
  75.3 85.9 %all-gather.2.cloned.1.call-done = f32[8,100,1024]{2,1,0:T(8,128)} async-done(((f32[2,100,1024]{2,1,0:T(8,128)}), f32[8,100,1024]{2,1,0:T(8,128)}) %all-gather.2.cloned.1.call-update) | async-done | bytes 3276816 | tf_op jit(solution)/shard_map/all_gather | solution.py:157
  161.2 3.2 fusion.195
  164.4 1.3 fusion.196
  165.7 1.1 fusion.197
  167.8 6.7 fusion.57
  174.5 3.5 pad_add_fusion
  178.0 1.4 fusion.37
  179.4 2.2 copy.104
  181.7 63.8 %scatter_fusion = f32[2,100,128]{1,0,2:T(2,128)S(1)} fusion(f32[2,100,128]{1,0,2:T(2,128)S(1)} %broadcast_in_dim.59, s32[1024]{0:T(1024)S(1)} %get-tuple-element.163, f32[1024,2,100]{2,1,0:T(2,128)} %copy.104), kind=kCustom, calls=%fused_computation.1 | custom fusion | flops 204800 | bytes 2461696 | tf_op jit(solution)/shard_map/transpose(jvp(jit(_take)))/scatter-add | solution.py:149
  246.0 0.8 copy-done.15
  246.8 3.2 bitcast_convert_fusion
  250.0 2.0 fusion.21
  252.3 95.8 %all-reduce.69.cloned.1.call-done = bf16[1024,1024]{1,0:T(8,128)(2,1)} async-done(((bf16[1024,1024]{1,0:T(8,128)(2,1)}), bf16[1024,1024]{1,0:T(8,128)(2,1)}) %all-reduce.69.cloned.1.call-update) | async-done | bytes 2097168 | tf_op jit(solution)/shard_map/psum | solution.py:197
  348.1 4.1 convert_element_type.189
  353.0 2.6 convolution_convert_fusion.7
  355.5 1.2 copy.106
  356.9 5.8 fusion.5
  362.8 5.8 convolution_convert_fusion.2
  368.6 1.6 copy.111
  371.2 1.6 copy.108
  372.8 1.1 copy-done.5
  373.9 3.0 fusion.23
  376.9 1.3 collective-permute-start.2
  378.2 4.2 collective-permute-start.3
  383.1 7.9 fusion.17
  391.0 79.1 %psum.21 = f32[]{:T(128)} all-reduce(f32[]{:T(128)S(6)} %div.254), channel_id=1, replica_groups=mesh['member'=4,'token'=64] {'member','token'}, use_global_device_ids=true, to_apply=%region_5.6 | all-reduce | flops 1 | bytes 8 | tf_op jit(solution)/shard_map/psum | solution.py:171
  470.7 1.8 fusion.27
  472.6 1.9 add_add_fusion.1
  474.4 1.6 fusion.224
  476.0 3.2 add_convert_fusion
  479.3 1.9 slice_convert_fusion
  481.1 2.1 reshape.877
  484.3 0.7 copy-done.45
  485.0 0.8 convolution_convert_fusion.6
  485.8 0.8 fusion.19
  486.9 1.2 fusion.26
  488.1 113.7 %all-reduce.71.cloned.1.call-done = f32[100,1024]{1,0:T(8,128)} async-done(((f32[100,1024]{1,0:T(8,128)}), f32[100,1024]{1,0:T(8,128)}) %all-reduce.71.cloned.1.call-update) | async-done | bytes 409616 | tf_op jit(solution)/shard_map/psum | solution.py:171
  601.8 300.7 %reduce-scatter.2.cloned.1.call-done = f32[16,1024]{1,0:T(8,128)} async-done(((f32[1024,1024]{1,0:T(8,128)}), f32[16,1024]{1,0:T(8,128)}) %reduce-scatter.2.cloned.1.call-update) | async-done | bytes 65552 | tf_op jit(solution)/shard_map/reduce_scatter | solution.py:198
  902.5 1.8 copy.143
  (129 shorter events, 8.8 us)
Async XLA Ops:
  7.2 48.1 %copy-start = (bf16[1024,1024]{1,0:T(8,128)(2,1)S(1)}, bf16[1024,1024]{1,0:T(8,128)(2,1)}, u32[]{:S(2)}) copy-start(bf16[1024,1024]{1,0:T(8,128)(2,1)} %param.27) | copy-start | bytes 6291460
  7.2 5.6 copy-start.8
  7.2 5.6 copy-start.7
  7.2 5.6 copy-start.41
  7.2 154.0 %all-gather.2.cloned.1.call-start = ((), (), s32[]{:S(2)}) async-start(), calls=%async_computation.1 | async-start | bytes 4259840 | tf_op jit(solution)/shard_map/all_gather | solution.py:157
  13.0 0.8 copy-start.26
  16.2 0.6 copy-start.35
  16.2 1.0 copy-start.9
  16.8 0.6 copy-start.30
  25.5 12.1 %copy-start.42 = (s32[1024]{0:T(1024)S(1)}, s32[1024]{0:T(1024)}, u32[]{:S(2)}) copy-start(s32[1024]{0:T(1024)} %param.33) | copy-start | bytes 12292
  29.3 11.2 %collective-permute-start = (bf16[2,2,128,1024]{2,1,3,0:T(2,128)(2,1)}, bf16[2,2,128,1024]{2,1,3,0:T(2,128)(2,1)}, u32[]{:S(2)}, u32[]{:S(2)}) collective-permute-start(bf16[2,2,128,1024]{2,1,3,0:T(2,128)(2,1)} %pad_maximum_fusion.1), channel_id=1, source_target_pairs={{0,1},{1,2},{2,3},{3,4},{4,5},{5,6},{6,7},{7,8},{8,9},{9,10},{10,1... | collective-permute-start | bytes 3145736 | tf_op jit(solution)/shard_map/ppermute | solution.py:17
  32.1 8.4 collective-permute-start.1
  37.6 3.2 copy-start.13
  37.6 3.2 copy-start.14
  40.3 0.6 copy-start.37
  40.3 8.9 copy-start.19
  40.3 8.9 copy-start.39
  40.4 10.6 %copy-start.28 = (pred[128,384]{1,0:T(8,128)(4,1)}, pred[128,384]{1,0:T(8,128)(4,1)S(1)}, u32[]{:S(2)}) copy-start(pred[128,384]{1,0:T(8,128)(4,1)S(1)} %and_and_fusion) | copy-start | bytes 147460
  49.0 2.0 copy-start.23
  49.2 4.5 copy-start.12
  51.0 2.7 copy-start.11
  51.0 2.7 copy-start.33
  53.7 2.3 copy-start.3
  55.2 0.8 copy-start.18
  55.2 1.6 copy-start.24
  55.2 1.6 copy-start.44
  56.0 0.8 copy-start.17
  57.8 103.4 %copy-start.32 = (f32[1024]{0:T(1024)S(1)}, f32[1024]{0:T(1024)}, u32[]{:S(2)}) copy-start(f32[1024]{0:T(1024)} %param.31) | copy-start | bytes 12292
  57.8 103.4 %copy-start.43 = (f32[100]{0:T(128)S(1)}, f32[100]{0:T(128)}, u32[]{:S(2)}) copy-start(f32[100]{0:T(128)} %param.32) | copy-start | bytes 1204
  74.7 273.4 %all-reduce.69.cloned.1.call-start = ((), (), s32[]{:S(2)}) async-start(), calls=%async_computation.2 | async-start | bytes 4194304 | tf_op jit(solution)/shard_map/psum | solution.py:197
  161.2 3.2 copy-start.2
  166.8 1.0 copy-start.27
  246.0 0.8 copy-start.15
  250.0 351.8 %all-reduce.71.cloned.1.call-start = ((), (), s32[]{:S(2)}) async-start(), calls=%async_computation.4 | async-start | bytes 851968 | tf_op jit(solution)/shard_map/psum | solution.py:171
  252.1 650.4 %reduce-scatter.2.cloned.1.call-start = ((), (), s32[]{:S(2)}) async-start(), calls=%async_computation.3 | async-start | bytes 4259840 | tf_op jit(solution)/shard_map/reduce_scatter | solution.py:198
  352.2 0.7 copy-start.34
  352.9 4.0 copy-start.29
  356.9 5.8 copy-start.20
  356.9 5.8 copy-start.40
  362.7 5.8 copy-start.47
  368.6 1.9 copy-start.4
  372.8 1.2 copy-start.5
  376.9 99.1 %collective-permute-start.2 = (bf16[2,2,128,1024]{2,1,3,0:T(2,128)(2,1)}, bf16[2,2,128,1024]{2,1,3,0:T(2,128)(2,1)}, u32[]{:S(2)}, u32[]{:S(2)}) collective-permute-start(bf16[2,2,128,1024]{2,1,3,0:T(2,128)(2,1)} %get-tuple-element.157), channel_id=1, source_target_pairs={{1,0},{2,1},{3,2},{4,3},{5,4},{6,5},{7,6},{8,7},{9,8},{10,9},{11,1... | collective-permute-start | bytes 3145736 | tf_op jit(solution)/shard_map/ppermute | solution.py:28
  378.2 97.8 %collective-permute-start.3 = (bf16[2,2,128,1024]{2,1,3,0:T(2,128)(2,1)}, bf16[2,2,128,1024]{2,1,3,0:T(2,128)(2,1)}, u32[]{:S(2)}, u32[]{:S(2)}) collective-permute-start(bf16[2,2,128,1024]{2,1,3,0:T(2,128)(2,1)} %get-tuple-element.158), channel_id=1, source_target_pairs={{0,1},{1,2},{2,3},{3,4},{4,5},{5,6},{6,7},{7,8},{8,9},{9,10},{10,1... | collective-permute-start | bytes 3145736 | tf_op jit(solution)/shard_map/ppermute | solution.py:28
  383.0 89.5 %copy-start.38 = (f32[256,16]{0,1:T(8,128)S(1)}, f32[256,16]{0,1:T(8,128)}, u32[]{:S(2)}) copy-start(f32[256,16]{0,1:T(8,128)} %copy-done.37) | copy-start | bytes 49156
  470.7 3.8 copy-start.21
  472.5 3.5 copy-start.6
  479.3 4.0 copy-start.10
  479.3 4.1 copy-start.36
  479.3 4.2 copy-start.31
  483.2 1.0 copy-start.25
  483.2 1.8 copy-start.45
  483.4 2.4 copy-start.22
  483.4 2.4 copy-start.46
  485.8 1.2 copy-start.16
  485.8 418.5 %copy-start.1 = (bf16[1024,1024]{1,0:T(8,128)(2,1)S(1)}, bf16[1024,1024]{1,0:T(8,128)(2,1)}, u32[]{:S(2)}) copy-start(bf16[1024,1024]{1,0:T(8,128)(2,1)} %param.27) | copy-start | bytes 6291460
Sparse Core Ops, SparseCore 0:
  74.8 86.3 all-gather.1
  250.1 97.9 all-reduce.68
  354.2 247.5 all-reduce.70
  604.7 297.7 reduce-scatter.1
where the time goes:
time: 922 us; the launch traced here: 912 us
  waiting for transfers between devices  596 us (65%)
  other arithmetic  119 us (13%)
  blocking collectives  79.1 us (9%)
  local copies, waits for them, and re-layouts  45.2 us (5%)
  matrix products  44.6 us (5%)
  between operations  17.3 us (2%)
  starting transfers between devices  10.7 us (1%)
    reduce_scatter x1, waiting for transfers between devices, shards(): lax.psum_scatter(summed, 'token', scatter_dimension=0, tiled=True)  301 us
    psum x1, waiting for transfers between devices, shards(): lax.psum((partial_loss, readout_piece_result), ('member', 'token'))  114 us
    psum x1, waiting for transfers between devices, shards(): lax.psum(product.astype(jnp.bfloat16), 'member').astype(jnp.float32)  95.8 us
    all_gather x1, waiting for transfers between devices, shards(): lax.all_gather(realization_prediction, 'member', axis=0, tiled=True)  85.9 us
    psum x1, blocking collectives, shards(): lax.psum((partial_loss, readout_piece_result), ('member', 'token'))  79.1 us
    scatter-add x1, other arithmetic, decode_tokens(): return jnp.take(mapping_array, point_map, axis=2)  63.8 us
    unnamed x99, local copies, waits for them, and re-layouts  18.8 us
  transfers between devices with their start and end apart: 8, of which 4 were waited for; matrix products, arithmetic and copies ran while one was open for 6% of the time, Pallas kernels for 0%

commit v1 on v0

--- a/solution.py
+++ b/solution.py
@@ -154,7 +154,12 @@
     location_places = realization_prediction.shape[2]
     groups = lax.axis_size("member")
     local_shard = lax.axis_index("member")
-    gathered_lines = lax.all_gather(realization_prediction, "member", axis=0, tiled=True)
+    gathered_lines = jnp.concatenate(
+        lax.all_to_all(
+            jnp.stack([realization_prediction] * lax.axis_size("member")), "member", 0, 0
+        ),
+        axis=0,
+    )
 
     def score_all(whole):
         return unbiased_ranked_score(

time: 922 us -> 890 us (0.965)
  other arithmetic: 119 us -> 86.1 us
    all_gather x1 -> x0, waiting for transfers between devices: 85.9 us -> none  [shards(): lax.all_gather(realization_prediction, 'member', axis=0, tiled=True)]
    all_to_all x0 -> x1, waiting for transfers between devices: none -> 50 us  [shards(): lax.all_to_all(jnp.stack([realization_prediction] * lax.axis_size('member...]
    psum x1, waiting for transfers between devices: 95.8 us -> 128 us  [shards(): lax.psum(product.astype(jnp.bfloat16), 'member').astype(jnp.float32)]
    scatter-add x1, other arithmetic: 63.8 us -> 33.1 us  [decode_tokens(): return jnp.take(mapping_array, point_map, axis=2)]
    unnamed x99 -> x105, local copies, waits for them, and re-layouts: 18.8 us -> 15.5 us
where the time goes in v1:
time: 890 us; the launch traced here: 886 us
  waiting for transfers between devices  599 us (67%)
  other arithmetic  86.1 us (10%)
  blocking collectives  79 us (9%)
  local copies, waits for them, and re-layouts  46.1 us (5%)
  matrix products  39.6 us (4%)
  starting transfers between devices  18.7 us (2%)
  between operations  17.4 us (2%)
    reduce_scatter x1, waiting for transfers between devices, shards(): lax.psum_scatter(summed, 'token', scatter_dimension=0, tiled=True)  301 us
    psum x1, waiting for transfers between devices, shards(): lax.psum(product.astype(jnp.bfloat16), 'member').astype(jnp.float32)  128 us
    psum x1, waiting for transfers between devices, shards(): lax.psum((partial_loss, readout_piece_result), ('member', 'token'))  120 us
    psum x1, blocking collectives, shards(): lax.psum((partial_loss, readout_piece_result), ('member', 'token'))  79 us
    all_to_all x1, waiting for transfers between devices, shards(): lax.all_to_all(jnp.stack([realization_prediction] * lax.axis_size('member...  50 us
    scatter-add x1, other arithmetic, decode_tokens(): return jnp.take(mapping_array, point_map, axis=2)  33.1 us
  transfers between devices with their start and end apart: 8, of which 4 were waited for; matrix products, arithmetic and copies ran while one was open for 6% of the time, Pallas kernels for 0%

profile of v1, /device:TPU:64, one launch (start us, length us, event | category | flops | bytes accessed | tf_op | source)
XLA Modules:
  0.0 885.5 jit_solution(18044666133952023573)
XLA Ops:
  7.2 1.6 multiply_reduce_fusion.3
  9.4 3.9 copy.70
  13.5 0.8 copy-done.26
  14.3 2.3 multiply_reduce_fusion.2
  16.7 1.0 copy-done.8
  17.7 0.9 multiply_convert_fusion.1
  18.6 2.0 convert_element_type.154
  20.6 3.3 convolution_convert_fusion.8
  23.8 2.0 copy.71
  25.8 3.8 pad_maximum_fusion.1
  29.6 2.7 collective-permute-start
  32.4 1.6 collective-permute-start.1
  34.0 4.0 copy.73
  38.6 2.5 multiply_reduce_fusion.1
  41.4 5.8 pad_maximum_fusion
  47.2 2.2 fusion.223
  49.9 1.8 fusion.7
  51.7 1.4 divide_convert_fusion
  53.1 1.5 convolution_convert_fusion.5
  54.7 0.7 fusion.13
  55.5 0.8 copy-done.16
  56.7 7.5 gather_fusion
  64.2 5.3 select_bitcast_fusion
  69.5 2.2 copy.78
  71.7 3.9 stack.5
  75.6 8.1 all-to-all-start
  84.3 50.0 %all-to-all-done = f32[4,2,100,1024]{3,1,2,0:T(2,128)} async-done(((f32[4,2,100,1024]{3,1,2,0:T(2,128)}), f32[4,2,100,1024]{3,1,2,0:T(2,128)}, u32[]{:S(2)}, u32[]{:S(2)}) %all-to-all-start) | async-done | bytes 3276832 | tf_op jit(solution)/shard_map/all_to_all | solution.py:158
  134.2 2.9 copy.79
  137.2 1.3 fusion.195
  138.5 1.3 fusion.196
  139.8 1.1 fusion.197
  141.9 6.7 fusion.57
  148.6 3.5 pad_add_fusion
  152.1 1.3 fusion.37
  153.5 1.5 copy.80
  155.0 33.1 %scatter_fusion = f32[2,100,128]{1,0,2:T(2,128)S(1)} fusion(f32[2,100,128]{1,0,2:T(2,128)S(1)} %broadcast_in_dim.59, s32[1024]{0:T(1024)} %get-tuple-element.163, f32[1024,2,100]{2,1,0:T(2,128)S(1)} %copy.80), kind=kCustom, calls=%fused_computation.1 | custom fusion | flops 204800 | bytes 2461696 | tf_op jit(solution)/shard_map/transpose(jvp(jit(_take)))/scatter-add | solution.py:149
  188.6 3.4 bitcast_convert_fusion
  192.1 1.0 fusion.21
  193.3 128.0 %all-reduce.69.cloned.1.call-done = bf16[1024,1024]{1,0:T(8,128)(2,1)} async-done(((bf16[1024,1024]{1,0:T(8,128)(2,1)}), bf16[1024,1024]{1,0:T(8,128)(2,1)}) %all-reduce.69.cloned.1.call-update) | async-done | bytes 2097168 | tf_op jit(solution)/shard_map/psum | solution.py:202
  321.3 4.1 convert_element_type.189
  326.1 1.5 convolution_convert_fusion.7
  327.7 1.4 copy.82
  329.2 5.9 fusion.5
  335.2 3.1 convolution_convert_fusion.2
  338.3 1.6 copy.87
  340.9 1.6 copy.84
  342.5 2.9 fusion.23
  345.5 1.3 collective-permute-start.2
  346.8 4.2 collective-permute-start.3
  351.6 8.0 fusion.17
  359.6 79.0 %psum.21 = f32[]{:T(128)} all-reduce(f32[]{:T(128)S(6)} %div.254), channel_id=1, replica_groups=mesh['member'=4,'token'=64] {'member','token'}, use_global_device_ids=true, to_apply=%region_5.6 | all-reduce | flops 1 | bytes 8 | tf_op jit(solution)/shard_map/psum | solution.py:176
  439.3 1.8 fusion.27
  441.2 1.7 add_add_fusion.1
  442.9 1.6 fusion.224
  444.5 3.2 add_convert_fusion
  447.7 1.5 slice_convert_fusion
  449.3 0.8 reshape.883
  451.2 0.7 copy-done.46
  451.9 0.8 convolution_convert_fusion.6
  452.7 0.8 fusion.19
  453.9 1.2 fusion.26
  455.1 119.9 %all-reduce.71.cloned.1.call-done = f32[100,1024]{1,0:T(8,128)} async-done(((f32[100,1024]{1,0:T(8,128)}), f32[100,1024]{1,0:T(8,128)}) %all-reduce.71.cloned.1.call-update) | async-done | bytes 409616 | tf_op jit(solution)/shard_map/psum | solution.py:176
  575.0 300.8 %reduce-scatter.2.cloned.1.call-done = f32[16,1024]{1,0:T(8,128)} async-done(((f32[1024,1024]{1,0:T(8,128)}), f32[16,1024]{1,0:T(8,128)}) %reduce-scatter.2.cloned.1.call-update) | async-done | bytes 65552 | tf_op jit(solution)/shard_map/reduce_scatter | solution.py:203
  875.9 1.8 copy.119
  (137 shorter events, 8.0 us)
Async XLA Ops:
  7.2 47.5 %copy-start = (bf16[1024,1024]{1,0:T(8,128)(2,1)S(1)}, bf16[1024,1024]{1,0:T(8,128)(2,1)}, u32[]{:S(2)}) copy-start(bf16[1024,1024]{1,0:T(8,128)(2,1)} %param.27) | copy-start | bytes 6291460
  7.2 6.1 copy-start.6
  7.2 6.1 copy-start.4
  7.2 6.1 copy-start.37
  8.8 0.5 copy-start.41
  9.4 4.2 copy-start.43
  13.5 0.8 copy-start.26
  16.7 1.0 copy-start.8
  16.7 9.2 %copy-start.31 = (f32[256,16]{0,1:T(8,128)}, f32[256,16]{0,1:T(8,128)S(1)}, u32[]{:S(2)}) copy-start(f32[256,16]{0,1:T(8,128)S(1)} %get-tuple-element.165) | copy-start | bytes 49156
  25.8 12.1 %copy-start.39 = (s32[1024]{0:T(1024)S(1)}, s32[1024]{0:T(1024)}, u32[]{:S(2)}) copy-start(s32[1024]{0:T(1024)} %param.33) | copy-start | bytes 12292
  29.6 11.7 %collective-permute-start = (bf16[2,2,128,1024]{2,1,3,0:T(2,128)(2,1)}, bf16[2,2,128,1024]{2,1,3,0:T(2,128)(2,1)}, u32[]{:S(2)}, u32[]{:S(2)}) collective-permute-start(bf16[2,2,128,1024]{2,1,3,0:T(2,128)(2,1)} %pad_maximum_fusion.1), channel_id=1, source_target_pairs={{0,1},{1,2},{2,3},{3,4},{4,5},{5,6},{6,7},{7,8},{8,9},{9,10},{10,1... | collective-permute-start | bytes 3145736 | tf_op jit(solution)/shard_map/ppermute | solution.py:17
  32.4 8.9 %collective-permute-start.1 = (bf16[2,2,128,1024]{2,1,3,0:T(2,128)(2,1)}, bf16[2,2,128,1024]{2,1,3,0:T(2,128)(2,1)}, u32[]{:S(2)}, u32[]{:S(2)}) collective-permute-start(bf16[2,2,128,1024]{2,1,3,0:T(2,128)(2,1)} %pad_maximum_fusion.1), channel_id=1, source_target_pairs={{1,0},{2,1},{3,2},{4,3},{5,4},{6,5},{7,6},{8,7},{9,8},{10,9},{11,1... | collective-permute-start | bytes 3145736 | tf_op jit(solution)/shard_map/ppermute | solution.py:20
  38.0 3.4 copy-start.12
  38.0 3.4 copy-start.13
  41.1 8.3 copy-start.33
  41.1 8.7 copy-start.19
  41.2 8.7 copy-start.35
  49.7 2.1 copy-start.23
  49.9 4.8 copy-start.11
  51.7 1.4 copy-start.29
  51.7 3.7 copy-start.10
  53.1 2.3 copy-start.2
  54.7 0.8 copy-start.18
  54.7 1.6 copy-start.24
  54.7 1.6 copy-start.45
  55.5 0.8 copy-start.16
  75.6 58.6 %all-to-all-start = ((f32[4,2,100,1024]{3,1,2,0:T(2,128)}), f32[4,2,100,1024]{3,1,2,0:T(2,128)}, u32[]{:S(2)}, u32[]{:S(2)}) async-start(f32[4,2,100,1024]{3,1,2,0:T(2,128)} %stack.5), calls=%async_computation | async-start | bytes 6553600 | tf_op jit(solution)/shard_map/all_to_all | solution.py:158
  83.7 53.4 %copy-start.28 = (f32[1024]{0:T(1024)S(1)}, f32[1024]{0:T(1024)}, u32[]{:S(2)}) copy-start(f32[1024]{0:T(1024)} %param.31) | copy-start | bytes 12292
  83.7 53.5 %copy-start.40 = (f32[100]{0:T(128)S(1)}, f32[100]{0:T(128)}, u32[]{:S(2)}) copy-start(f32[100]{0:T(128)} %param.32) | copy-start | bytes 1204
  83.7 237.5 %all-reduce.69.cloned.1.call-start = ((), (), s32[]{:S(2)}) async-start(), calls=%async_computation.2 | async-start | bytes 4194304 | tf_op jit(solution)/shard_map/psum | solution.py:202
  140.9 1.0 copy-start.27
  188.1 4.0 copy-start.17
  188.6 137.6 %copy-start.14 = (bf16[2,128,1024]{2,1,0:T(8,128)(2,1)}, bf16[2,128,1024]{2,1,0:T(8,128)(2,1)S(1)}, u32[]{:S(2)}) copy-start(bf16[2,128,1024]{2,1,0:T(8,128)(2,1)S(1)} %convolution_convert_fusion.10) | copy-start | bytes 1572868
  192.0 383.0 %all-reduce.71.cloned.1.call-start = ((), (), s32[]{:S(2)}) async-start(), calls=%async_computation.4 | async-start | bytes 851968 | tf_op jit(solution)/shard_map/psum | solution.py:176
  193.1 682.8 %reduce-scatter.2.cloned.1.call-start = ((), (), s32[]{:S(2)}) async-start(), calls=%async_computation.3 | async-start | bytes 4259840 | tf_op jit(solution)/shard_map/reduce_scatter | solution.py:203
  325.4 0.7 copy-start.30
  327.7 7.4 slice-start
  329.2 5.9 slice-start.1
  329.2 5.9 copy-start.20
  329.2 5.9 copy-start.36
  335.1 3.2 copy-start.48
  338.3 1.9 copy-start.3
  345.5 99.0 %collective-permute-start.2 = (bf16[2,2,128,1024]{2,1,3,0:T(2,128)(2,1)}, bf16[2,2,128,1024]{2,1,3,0:T(2,128)(2,1)}, u32[]{:S(2)}, u32[]{:S(2)}) collective-permute-start(bf16[2,2,128,1024]{2,1,3,0:T(2,128)(2,1)} %get-tuple-element.157), channel_id=1, source_target_pairs={{1,0},{2,1},{3,2},{4,3},{5,4},{6,5},{7,6},{8,7},{9,8},{10,9},{11,1... | collective-permute-start | bytes 3145736 | tf_op jit(solution)/shard_map/ppermute | solution.py:28
  346.8 97.7 %collective-permute-start.3 = (bf16[2,2,128,1024]{2,1,3,0:T(2,128)(2,1)}, bf16[2,2,128,1024]{2,1,3,0:T(2,128)(2,1)}, u32[]{:S(2)}, u32[]{:S(2)}) collective-permute-start(bf16[2,2,128,1024]{2,1,3,0:T(2,128)(2,1)} %get-tuple-element.158), channel_id=1, source_target_pairs={{0,1},{1,2},{2,3},{3,4},{4,5},{5,6},{6,7},{7,8},{8,9},{9,10},{10,1... | collective-permute-start | bytes 3145736 | tf_op jit(solution)/shard_map/ppermute | solution.py:28
  351.6 89.5 %copy-start.34 = (f32[256,16]{0,1:T(8,128)S(1)}, f32[256,16]{0,1:T(8,128)}, u32[]{:S(2)}) copy-start(f32[256,16]{0,1:T(8,128)} %copy-done.33) | copy-start | bytes 49156
  439.3 3.6 copy-start.21
  447.7 2.4 copy-start.9
  447.7 2.6 copy-start.32
  450.1 1.0 copy-start.25
  450.1 1.8 copy-start.46
  450.3 2.4 copy-start.22
  450.3 2.4 copy-start.47
  451.9 1.7 copy-start.5
  451.9 1.7 copy-start.7
  451.9 1.7 copy-start.38
  452.7 1.2 copy-start.42
  452.7 1.2 copy-start.15
  452.7 1.2 copy-start.44
  452.7 424.9 %copy-start.1 = (bf16[1024,1024]{1,0:T(8,128)(2,1)S(1)}, bf16[1024,1024]{1,0:T(8,128)(2,1)}, u32[]{:S(2)}) copy-start(bf16[1024,1024]{1,0:T(8,128)(2,1)} %param.27) | copy-start | bytes 6291460
Sparse Core Ops, SparseCore 0:
  192.1 129.1 all-reduce.68
  327.4 247.6 all-reduce.70
  578.1 297.7 reduce-scatter.1
